TPU v7x, 1024 devices: a whole 4x8x16 slice. The times are simulated.
1024 devices in a mesh: ctx: 128 (over z_lo, y, x), tp: 8 (over z_hi, core).
Axes of the slice: x: 4, y: 8, z: 16 (z_hi: 4, z_lo: 4; z = z_hi * 4 + z_lo), core: 2. Of those that a mesh axis runs over, the one named last changes fastest.
Arguments:
- projected: bfloat16 [3, 4096, 16384], P(None, 'tp', 'ctx'), may hold values from -6 to 6
- short_taps: bfloat16 [3, 7, 4096], P(None, None, 'tp'), may hold values from -2 to 2
- long_filter: float32 [4096, 16384], P(('tp', 'ctx')), may hold values from -1.1 to 1.1
- out_weight: bfloat16 [4096, 4096], P('tp'), may hold values from -0.09375 to 0.09375
- residual: bfloat16 [16384, 4096], P('ctx'), may hold values from -60 to 60
- norm_gain: float32 [4096], P('tp'), may hold values from 0.25 to 1.75
Outputs:
- residual_out: bfloat16 [16384, 4096], P('ctx', 'tp')
- normed_out: bfloat16 [16384, 4096], P('ctx', 'tp')
All inputs are finite; a program needn't handle non-finite values.
Results may differ from a plain program's by a relative error of at most 0.014.
Values may be sent and summed in bfloat16 or wider, within the bound.
No kernel may reach another device: no remote copies, remote signals or barrier semaphores. Data moves between devices by JAX's collectives and lax.ppermute only.
A program may use at most 32 MiB of HBM per device.

v0:
```python
import math

import jax
import jax.numpy as jnp
from jax import lax
from jax.sharding import PartitionSpec as P

epsilon = 1e-06
highest = lax.Precision.HIGHEST


def passed_along(block, axis, distance):
    devices = range(lax.axis_size(axis))
    route = [(i - distance, i) for i in devices if i - distance in devices]
    return lax.ppermute(block, axis, route)


def angle_table(row_count, col_count, period):
    row_index = lax.iota(jnp.int32, row_count)[:, None]
    col_index = lax.iota(jnp.int32, col_count)[None, :]
    phase_int = row_index * col_index % period
    angles = phase_int.astype(jnp.float32) * (2.0 * math.pi / period)
    return (jnp.cos(angles), jnp.sin(angles))


def contract(form, first_arg, second_arg):
    return jnp.einsum(form, first_arg, second_arg, precision=highest)


def forward_dft(signal, tables):
    first_cos, first_sin, twist_cos, twist_sin, inner_cos, inner_sin = tables
    real_one = contract("cma,mk->cka", signal, first_cos)
    imag_one = -contract("cma,mk->cka", signal, first_sin)
    real_two = real_one * twist_cos + imag_one * twist_sin
    imag_two = imag_one * twist_cos - real_one * twist_sin
    real_out = contract("cka,aj->ckj", real_two, inner_cos) + contract(
        "cka,aj->ckj", imag_two, inner_sin
    )
    imag_out = contract("cka,aj->ckj", imag_two, inner_cos) - contract(
        "cka,aj->ckj", real_two, inner_sin
    )
    return (real_out, imag_out)


def inverse_dft(real_in, imag_in, tables, length_total):
    first_cos, first_sin, twist_cos, twist_sin, inner_cos, inner_sin = tables
    real_one = contract("ckj,ja->cka", real_in, inner_cos) - contract(
        "ckj,ja->cka", imag_in, inner_sin
    )
    imag_one = contract("ckj,ja->cka", imag_in, inner_cos) + contract(
        "ckj,ja->cka", real_in, inner_sin
    )
    real_two = real_one * twist_cos - imag_one * twist_sin
    imag_two = imag_one * twist_cos + real_one * twist_sin
    signal = contract("mk,cka->cma", first_cos, real_two) - contract(
        "mk,cka->cma", first_sin, imag_two
    )
    return signal / length_total


def body(projected, short_taps, long_filter, out_weight, residual, norm_gain):
    tap_count = short_taps.shape[1]
    tok_rows = projected.shape[2]
    rim_rows = passed_along(projected[:, :, tok_rows - (tap_count - 1) :], "ctx", 1)
    extended = jnp.concatenate([rim_rows, projected], axis=2)
    shaped = jnp.zeros(projected.shape, jnp.float32)
    for tap_index in range(tap_count):
        window_rows = extended[:, :, tap_index : tap_index + tok_rows].astype(jnp.float32)
        shaped = shaped + short_taps[:, tap_index, :].astype(jnp.float32)[:, :, None] * window_rows
    product = (shaped[1] * shaped[2]).astype(jnp.bfloat16)
    spread = lax.all_to_all(product, "ctx", split_axis=0, concat_axis=1, tiled=True)
    ctx_count = lax.axis_size("ctx")
    full_m = 2 * ctx_count
    length_total = tok_rows * full_m
    first_cos, first_sin = angle_table(ctx_count, full_m, full_m)
    twist_cos, twist_sin = angle_table(full_m, tok_rows, length_total)
    inner_cos, inner_sin = angle_table(tok_rows, tok_rows, tok_rows)
    tables = (first_cos, first_sin, twist_cos, twist_sin, inner_cos, inner_sin)
    conv_ch = spread.shape[0]
    signal = spread.astype(jnp.float32).reshape(conv_ch, ctx_count, tok_rows)
    filter_rows = long_filter.reshape(conv_ch, ctx_count, tok_rows)
    signal_real, signal_imag = forward_dft(signal, tables)
    filter_real, filter_imag = forward_dft(filter_rows, tables)
    spectrum_real = signal_real * filter_real - signal_imag * filter_imag
    spectrum_imag = signal_real * filter_imag + signal_imag * filter_real
    filtered = inverse_dft(spectrum_real, spectrum_imag, tables, length_total)
    conv = filtered.reshape(conv_ch, ctx_count * tok_rows).astype(jnp.bfloat16)
    returned = lax.all_to_all(conv, "ctx", split_axis=1, concat_axis=0, tiled=True)
    gated = (shaped[0] * returned.astype(jnp.float32)).astype(jnp.bfloat16)
    partial_value = lax.dot_general(
        gated, out_weight, (((0,), (0,)), ((), ())), preferred_element_type=jnp.float32
    )
    group_ch = out_weight.shape[0]
    start_col = lax.axis_index("tp") * group_ch
    gain_row = norm_gain[None, :]
    totals = lax.psum(partial_value.astype(jnp.bfloat16), "tp").astype(jnp.float32)
    summed = residual.astype(jnp.float32) + totals
    inverse_rms = lax.rsqrt(jnp.mean(summed * summed, axis=1) + epsilon)
    own_rows = lax.dynamic_slice_in_dim(summed, start_col, group_ch, 1)
    residual_out = own_rows.astype(jnp.bfloat16)
    normed_out = (own_rows * inverse_rms[:, None] * gain_row).astype(jnp.bfloat16)
    return (residual_out, normed_out)


def solution(mesh):
    placed = (
        P(None, "tp", "ctx"),
        P(None, None, "tp"),
        P(("tp", "ctx"), None),
        P("tp", None),
        P("ctx", None),
        P("tp"),
    )
    return jax.shard_map(
        body,
        mesh=mesh,
        in_specs=placed,
        out_specs=(P("ctx", "tp"), P("ctx", "tp")),
        check_vma=False,
    )
```

profile of v0, /device:TPU:1, one launch (start us, length us, event | category | flops | bytes accessed | tf_op | source)
XLA Modules:
  0.0 211.9 jit_solution(4261883533613436724)
XLA Ops:
  7.2 1.2 slice.52
  8.4 4.0 %collective-permute-start = (bf16[3,512,6]{2,1,0:T(8,128)(2,1)S(1)}, bf16[3,512,6]{2,1,0:T(8,128)(2,1)S(1)}, u32[]{:S(2)}, u32[]{:S(2)}) collective-permute-start(bf16[3,512,6]{2,1,0:T(8,128)(2,1)S(1)} %slice.52), channel_id=1, source_target_pairs={{0,8},{8,16},{16,24},{24,32},{32,40},{40,48},{48,56},{56,64},{64,7... | collective-permute-start | bytes 55304 | tf_op jit(solution)/shard_map/ppermute | solution.py:15
  12.3 0.5 fusion.82
  12.9 2.0 convolution_negate_fusion
  14.9 2.0 fusion.28
  17.0 0.8 fusion.3
  17.8 0.8 convolution_subtract_fusion.1
  18.8 2.9 %multiply_add_fusion = f32[3,512,128]{2,1,0:T(8,128)S(1)} fusion(bf16[3,512,128]{2,1,0:T(8,128)(2,1)S(1)} %copy-done, bf16[3,512,6]{2,1,0:T(8,128)(2,1)S(1)} %collective-permute-done, f32[3,512]{1,0:T(4,128)S(1)} %get-tuple-element.15, f32[3,512]{1,0:T(4,128)S(1)} %get-tuple-element.16, f32[3,512]{1,0:T(4,128)S(1)} %get-tuple-element.17, ...), kind=kLoop, calls=%fused_computation.25 | loop fusion | flops 7471104 | bytes 1241088 | tf_op jit(solution)/shard_map/add | solution.py:69
  21.6 0.7 fusion.30
  22.3 20.1 %all-to-all-start = ((bf16[128,4,128]{2,1,0:T(4,128)(2,1)}), bf16[128,4,128]{2,1,0:T(4,128)(2,1)S(1)}, u32[]{:S(2)}, u32[]{:S(2)}) async-start(bf16[128,4,128]{2,1,0:T(4,128)(2,1)} %bitcast.2), calls=%async_computation | async-start | bytes 262144 | tf_op jit(solution)/shard_map/all_to_all | solution.py:71
  42.4 0.2 all-reduce.2.cloned.1.call-start
  42.6 0.8 fusion.7
  43.5 0.8 convolution_add_fusion.1
  44.3 9.5 %all-to-all-done = bf16[128,4,128]{2,1,0:T(4,128)(2,1)S(1)} async-done(((bf16[128,4,128]{2,1,0:T(4,128)(2,1)}), bf16[128,4,128]{2,1,0:T(4,128)(2,1)S(1)}, u32[]{:S(2)}, u32[]{:S(2)}) %all-to-all-start) | async-done | bytes 131104 | tf_op jit(solution)/shard_map/all_to_all | solution.py:71
  53.8 0.9 convolution_negate_fusion.1
  54.7 0.9 fusion.50
  55.5 0.8 fusion.9
  56.4 0.8 fusion.13
  57.2 0.8 convolution_add_fusion.2
  58.0 0.9 multiply_subtract_fusion
  58.9 0.8 fusion.74
  59.7 0.8 fusion.72
  60.6 0.8 convolution_subtract_fusion
  61.4 0.8 convolution_add_fusion
  62.2 1.4 fusion.18
  63.6 1.6 fusion.2
  65.4 17.0 %all_to_all.23 = bf16[4,128,128]{2,0,1:T(4,128)(2,1)S(1)} all-to-all(bf16[4,128,128]{2,0,1:T(4,128)(2,1)S(1)} %copy.29), channel_id=1, replica_groups=mesh['ctx'=128,'tp'=8] {'ctx'}, dimensions={1} | all-to-all | bytes 262144 | tf_op jit(solution)/shard_map/all_to_all | solution.py:88
  82.4 4.0 %convolution_convert_fusion = bf16[128,4096]{1,0:T(8,128)(2,1)} fusion(bf16[512,4096]{1,0:T(8,128)(2,1)} %param.9, f32[512,128]{1,0:T(8,128)S(1)} %bitcast.114, f32[3,512,128]{2,1,0:T(8,128)S(1)} %multiply_add_fusion), kind=kOutput, calls=%fused_computation | convolution fusion | flops 537526272 | bytes 5767168 | tf_op jit(solution)/shard_map/dot_general | solution.py:90
  86.5 115.4 %all-reduce.2.cloned.1.call-done = bf16[128,4096]{1,0:T(8,128)(2,1)} async-done(((bf16[128,4096]{1,0:T(8,128)(2,1)}), bf16[128,4096]{1,0:T(8,128)(2,1)}) %all-reduce.2.cloned.1.call-update) | async-done | bytes 1048592 | tf_op jit(solution)/shard_map/psum | solution.py:96
  201.9 1.7 multiply_reduce_fusion
  203.6 0.7 dynamic-slice_convert_fusion
  204.3 0.7 multiply_convert_fusion
  (18 shorter events, 0.3 us)
Async XLA Ops:
  7.2 9.8 %copy-start.2 = (bf16[3,7,512]{2,1,0:T(8,128)(2,1)S(1)}, bf16[3,7,512]{2,1,0:T(8,128)(2,1)}, u32[]{:S(2)}) copy-start(bf16[3,7,512]{2,1,0:T(8,128)(2,1)} %param.7) | copy-start | bytes 64516
  8.4 10.4 %collective-permute-start = (bf16[3,512,6]{2,1,0:T(8,128)(2,1)S(1)}, bf16[3,512,6]{2,1,0:T(8,128)(2,1)S(1)}, u32[]{:S(2)}, u32[]{:S(2)}) collective-permute-start(bf16[3,512,6]{2,1,0:T(8,128)(2,1)S(1)} %slice.52), channel_id=1, source_target_pairs={{0,8},{8,16},{16,24},{24,32},{32,40},{40,48},{48,56},{56,64},{64,7... | collective-permute-start | bytes 55304 | tf_op jit(solution)/shard_map/ppermute | solution.py:15
  17.0 1.7 copy-start
  22.3 31.5 %all-to-all-start = ((bf16[128,4,128]{2,1,0:T(4,128)(2,1)}), bf16[128,4,128]{2,1,0:T(4,128)(2,1)S(1)}, u32[]{:S(2)}, u32[]{:S(2)}) async-start(bf16[128,4,128]{2,1,0:T(4,128)(2,1)} %bitcast.2), calls=%async_computation | async-start | bytes 262144 | tf_op jit(solution)/shard_map/all_to_all | solution.py:71
  42.4 159.5 %all-reduce.2.cloned.1.call-start = ((), (), s32[]{:S(2)}) async-start(), calls=%async_computation.2 | async-start | bytes 2097152 | tf_op jit(solution)/shard_map/psum | solution.py:96
  82.4 119.5 %copy-start.1 = (bf16[128,4096]{1,0:T(8,128)(2,1)S(1)}, bf16[128,4096]{1,0:T(8,128)(2,1)}, u32[]{:S(2)}) copy-start(bf16[128,4096]{1,0:T(8,128)(2,1)} %param.10) | copy-start | bytes 3145732
  86.5 117.8 %copy-start.3 = (f32[512]{0:T(512)S(1)}, f32[512]{0:T(512)}, u32[]{:S(2)}) copy-start(f32[512]{0:T(512)} %param.11) | copy-start | bytes 6148
Sparse Core Ops, SparseCore 0:
  86.6 115.2 all-reduce.1
where the time goes:
time: 212 us
  waiting for transfers between devices  125 us (59%)
  starting transfers between devices  24.3 us (11%)
  matrix products  22.8 us (11%)
  blocking collectives  17 us (8%)
  between operations  14.3 us (7%)
  other arithmetic  6.55 us (3%)
    psum x1, waiting for transfers between devices, body(): lax.psum(partial_value.astype(jnp.bfloat16), 'tp').astype(jnp.float32)  115 us
    all_to_all x1, starting transfers between devices, body(): lax.all_to_all(product, 'ctx', split_axis=0, concat_axis=1, tiled=True)  20.1 us
    dot_general x18, matrix products, contract(): return jnp.einsum(form, first_arg, second_arg, precision=highest)  18.8 us
    all_to_all x1, blocking collectives, body(): lax.all_to_all(conv, 'ctx', split_axis=1, concat_axis=0, tiled=True)  17 us
    all_to_all x1, waiting for transfers between devices, body(): lax.all_to_all(product, 'ctx', split_axis=0, concat_axis=1, tiled=True)  9.47 us
  transfers between devices with their start and end apart: 3, of which 2 were waited for; matrix products, arithmetic and copies ran while one was open for 4% of the time, Pallas kernels for 0%

commit v1 on v0

--- a/solution.py
+++ b/solution.py
@@ -3,9 +3,11 @@
 import jax
 import jax.numpy as jnp
 from jax import lax
-from jax.sharding import PartitionSpec as P
+from jax.sharding import Mesh, PartitionSpec as P
 
 epsilon = 1e-06
+REDUCE_MODE = "flat"
+TP_AXES = "tp"
 highest = lax.Precision.HIGHEST
 
 
@@ -90,31 +92,48 @@
     partial_value = lax.dot_general(
         gated, out_weight, (((0,), (0,)), ((), ())), preferred_element_type=jnp.float32
     )
+    tok_count, col_count = partial_value.shape
     group_ch = out_weight.shape[0]
-    start_col = lax.axis_index("tp") * group_ch
-    gain_row = norm_gain[None, :]
-    totals = lax.psum(partial_value.astype(jnp.bfloat16), "tp").astype(jnp.float32)
-    summed = residual.astype(jnp.float32) + totals
-    inverse_rms = lax.rsqrt(jnp.mean(summed * summed, axis=1) + epsilon)
-    own_rows = lax.dynamic_slice_in_dim(summed, start_col, group_ch, 1)
+    if REDUCE_MODE == "flat":
+        own_part = lax.psum_scatter(
+            partial_value.astype(jnp.bfloat16), TP_AXES, scatter_dimension=1, tiled=True
+        )
+    else:
+        zh_count = lax.axis_size("zh")
+        co_count = lax.axis_size("co")
+        blocks = partial_value.astype(jnp.bfloat16).reshape(tok_count, zh_count, co_count, group_ch)
+        blocks = blocks.transpose(0, 2, 1, 3).reshape(tok_count, col_count)
+        half_part = lax.psum_scatter(blocks, "co", scatter_dimension=1, tiled=True)
+        own_part = lax.psum_scatter(half_part, "zh", scatter_dimension=1, tiled=True)
+    start_col = lax.axis_index(TP_AXES) * group_ch
+    own_res = lax.dynamic_slice_in_dim(residual, start_col, group_ch, 1)
+    own_rows = own_res.astype(jnp.float32) + own_part.astype(jnp.float32)
+    square_sum = lax.psum(jnp.sum(own_rows * own_rows, axis=1), TP_AXES)
+    inverse_rms = lax.rsqrt(square_sum / col_count + epsilon)
     residual_out = own_rows.astype(jnp.bfloat16)
-    normed_out = (own_rows * inverse_rms[:, None] * gain_row).astype(jnp.bfloat16)
+    normed_out = (own_rows * inverse_rms[:, None] * norm_gain[None, :]).astype(jnp.bfloat16)
     return (residual_out, normed_out)
 
 
 def solution(mesh):
+    tp_spec = TP_AXES
     placed = (
-        P(None, "tp", "ctx"),
-        P(None, None, "tp"),
-        P(("tp", "ctx"), None),
-        P("tp", None),
+        P(None, tp_spec, "ctx"),
+        P(None, None, tp_spec),
+        P((tp_spec, "ctx") if isinstance(tp_spec, str) else (*tp_spec, "ctx"), None),
+        P(tp_spec, None),
         P("ctx", None),
-        P("tp"),
+        P(tp_spec),
     )
+    if isinstance(tp_spec, str):
+        run_mesh = mesh
+    else:
+        ctx_count, tp_count = mesh.devices.shape
+        run_mesh = Mesh(mesh.devices.reshape(ctx_count, tp_count // 2, 2), ("ctx", "zh", "co"))
     return jax.shard_map(
         body,
-        mesh=mesh,
+        mesh=run_mesh,
         in_specs=placed,
-        out_specs=(P("ctx", "tp"), P("ctx", "tp")),
+        out_specs=(P("ctx", tp_spec), P("ctx", tp_spec)),
         check_vma=False,
     )

time: 212 us -> 178 us (0.84)
  waiting for transfers between devices: 125 us -> 71 us
  blocking collectives: 17 us -> 37.2 us
    psum x1 -> x0, waiting for transfers between devices: 115 us -> none  [body(): lax.psum(partial_value.astype(jnp.bfloat16), 'tp').astype(jnp.float32)]
    reduce_scatter x0 -> x1, waiting for transfers between devices: none -> 61.6 us  [body(): lax.psum_scatter(partial_value.astype(jnp.bfloat16), TP_AXES, scatter_dim...]
    psum x0 -> x1, blocking collectives: none -> 20.2 us  [body(): square_sum = lax.psum(jnp.sum(own_rows * own_rows, axis=1), TP_AXES)]
  transfers between devices with their start and end apart: 3 -> 3, of which waited for: 2 -> 2; matrix products, arithmetic and copies ran while one was open for 4% -> 5% of each run, Pallas kernels for 0% -> 0%
where the time goes in v1:
time: 178 us
  waiting for transfers between devices  71 us (40%)
  blocking collectives  37.2 us (21%)
  starting transfers between devices  23.3 us (13%)
  matrix products  22.7 us (13%)
  between operations  14.3 us (8%)
  other arithmetic  7.96 us (4%)
    reduce_scatter x1, waiting for transfers between devices, body(): lax.psum_scatter(partial_value.astype(jnp.bfloat16), TP_AXES, scatter_dim...  61.6 us
    psum x1, blocking collectives, body(): square_sum = lax.psum(jnp.sum(own_rows * own_rows, axis=1), TP_AXES)  20.2 us
    all_to_all x1, starting transfers between devices, body(): lax.all_to_all(product, 'ctx', split_axis=0, concat_axis=1, tiled=True)  19.1 us
    dot_general x18, matrix products, contract(): return jnp.einsum(form, first_arg, second_arg, precision=highest)  18.8 us
    all_to_all x1, blocking collectives, body(): lax.all_to_all(conv, 'ctx', split_axis=1, concat_axis=0, tiled=True)  17 us
    all_to_all x1, waiting for transfers between devices, body(): lax.all_to_all(product, 'ctx', split_axis=0, concat_axis=1, tiled=True)  9.46 us
    ppermute x1, starting transfers between devices, passed_along(): return lax.ppermute(block, axis, route)  3.96 us
    dot_general x1, matrix products, body(): lax.dot_general(gated, out_weight, (((0,), (0,)), ((), ())), preferred_el...  3.91 us
  transfers between devices with their start and end apart: 3, of which 2 were waited for; matrix products, arithmetic and copies ran while one was open for 5% of the time, Pallas kernels for 0%

profile of v1, /device:TPU:1, one launch (start us, length us, event | category | flops | bytes accessed | tf_op | source)
XLA Modules:
  0.0 177.8 jit_solution(13831296013533295020)
XLA Ops:
  7.2 1.2 slice.52
  8.4 4.0 %collective-permute-start = (bf16[3,512,6]{2,1,0:T(8,128)(2,1)S(1)}, bf16[3,512,6]{2,1,0:T(8,128)(2,1)S(1)}, u32[]{:S(2)}, u32[]{:S(2)}) collective-permute-start(bf16[3,512,6]{2,1,0:T(8,128)(2,1)S(1)} %slice.52), channel_id=1, source_target_pairs={{0,8},{8,16},{16,24},{24,32},{32,40},{40,48},{48,56},{56,64},{64,7... | collective-permute-start | bytes 55304 | tf_op jit(solution)/shard_map/ppermute | solution.py:17
  12.4 0.5 fusion.83
  12.9 2.0 %convolution_negate_fusion = f32[256,4,128]{2,0,1:T(8,128)S(1)} fusion(f32[1,4,128,128]{3,1,2,0:T(4,128)} %bitcast.112), kind=kOutput, calls=%fused_computation.1 | convolution fusion | flops 201916416 | bytes 786432 | tf_op jit(solution)/shard_map/cma,mk->cka/dot_general | solution.py:29
  15.0 2.0 %fusion.28 = f32[256,4,128]{2,0,1:T(8,128)S(1)} fusion(f32[1,4,128,128]{3,1,2,0:T(4,128)} %bitcast.113), kind=kOutput, calls=%fused_computation.56 | convolution fusion | flops 201785344 | bytes 786432 | tf_op jit(solution)/shard_map/cma,mk->cka/dot_general | solution.py:29
  17.0 1.0 slice_convert_fusion.6
  18.0 0.8 fusion.3
  18.9 0.8 convolution_subtract_fusion.1
  19.8 2.9 %multiply_add_fusion = f32[3,512,128]{2,1,0:T(8,128)S(1)} fusion(bf16[3,512,128]{2,1,0:T(8,128)(2,1)S(1)} %copy-done, bf16[3,512,6]{2,1,0:T(8,128)(2,1)S(1)} %collective-permute-done, f32[3,512]{1,0:T(4,128)S(1)} %get-tuple-element.15, f32[3,512]{1,0:T(4,128)S(1)} %get-tuple-element.16, f32[3,512]{1,0:T(4,128)S(1)} %get-tuple-element.17, ...), kind=kLoop, calls=%fused_computation.23 | loop fusion | flops 7471104 | bytes 1241088 | tf_op jit(solution)/shard_map/add | solution.py:71
  22.7 0.7 fusion.30
  23.3 19.1 %all-to-all-start = ((bf16[128,4,128]{2,1,0:T(4,128)(2,1)}), bf16[128,4,128]{2,1,0:T(4,128)(2,1)S(1)}, u32[]{:S(2)}, u32[]{:S(2)}) async-start(bf16[128,4,128]{2,1,0:T(4,128)(2,1)} %bitcast.2), calls=%async_computation | async-start | bytes 262144 | tf_op jit(solution)/shard_map/all_to_all | solution.py:73
  42.7 0.8 fusion.7
  43.5 0.8 convolution_add_fusion.1
  44.4 9.5 %all-to-all-done = bf16[128,4,128]{2,1,0:T(4,128)(2,1)S(1)} async-done(((bf16[128,4,128]{2,1,0:T(4,128)(2,1)}), bf16[128,4,128]{2,1,0:T(4,128)(2,1)S(1)}, u32[]{:S(2)}, u32[]{:S(2)}) %all-to-all-start) | async-done | bytes 131104 | tf_op jit(solution)/shard_map/all_to_all | solution.py:73
  53.8 0.9 convolution_negate_fusion.1
  54.7 0.9 fusion.51
  55.6 0.8 fusion.9
  56.4 0.8 fusion.13
  57.3 0.8 convolution_add_fusion.2
  58.1 0.9 multiply_subtract_fusion
  59.0 0.8 fusion.75
  59.8 0.8 fusion.73
  60.6 0.8 convolution_subtract_fusion
  61.5 0.8 convolution_add_fusion
  62.3 1.4 fusion.18
  63.7 1.6 fusion.2
  65.5 17.0 %all_to_all.23 = bf16[4,128,128]{2,0,1:T(4,128)(2,1)S(1)} all-to-all(bf16[4,128,128]{2,0,1:T(4,128)(2,1)S(1)} %copy.29), channel_id=1, replica_groups=mesh['ctx'=128,'tp'=8] {'ctx'}, dimensions={1} | all-to-all | bytes 262144 | tf_op jit(solution)/shard_map/all_to_all | solution.py:90
  82.5 3.9 %convolution_convert_fusion = bf16[128,4096]{1,0:T(8,128)(2,1)} fusion(bf16[512,4096]{1,0:T(8,128)(2,1)} %param.9, f32[512,128]{1,0:T(8,128)S(1)} %bitcast.114, f32[3,512,128]{2,1,0:T(8,128)S(1)} %multiply_add_fusion), kind=kOutput, calls=%fused_computation | convolution fusion | flops 537526272 | bytes 5767168 | tf_op jit(solution)/shard_map/dot_general | solution.py:92
  86.4 61.6 %reduce-scatter.2.cloned.1.call-done = bf16[128,512]{1,0:T(8,128)(2,1)} async-done(((bf16[128,4096]{1,0:T(8,128)(2,1)}), bf16[128,512]{1,0:T(8,128)(2,1)}) %reduce-scatter.2.cloned.1.call-update) | async-done | bytes 131088 | tf_op jit(solution)/shard_map/reduce_scatter | solution.py:98
  148.0 1.1 multiply_reduce_fusion
  149.1 20.2 %psum.7 = f32[128]{0:T(128)S(1)} all-reduce(f32[128]{0:T(128)S(1)} %multiply_reduce_fusion), channel_id=1, replica_groups=mesh['ctx'=128,'tp'=8] {'tp'}, use_global_device_ids=true, to_apply=%region_2.3 | all-reduce | flops 128 | bytes 1024 | tf_op jit(solution)/shard_map/psum | solution.py:111
  169.3 1.7 multiply_convert_fusion
  (14 shorter events, 0.5 us)
Async XLA Ops:
  7.2 12.6 %copy-start = (bf16[3,512,128]{2,1,0:T(8,128)(2,1)S(1)}, bf16[3,512,128]{2,1,0:T(8,128)(2,1)}, u32[]{:S(2)}) copy-start(bf16[3,512,128]{2,1,0:T(8,128)(2,1)} %param.6) | copy-start | bytes 1179652
  8.4 11.4 %collective-permute-start = (bf16[3,512,6]{2,1,0:T(8,128)(2,1)S(1)}, bf16[3,512,6]{2,1,0:T(8,128)(2,1)S(1)}, u32[]{:S(2)}, u32[]{:S(2)}) collective-permute-start(bf16[3,512,6]{2,1,0:T(8,128)(2,1)S(1)} %slice.52), channel_id=1, source_target_pairs={{0,8},{8,16},{16,24},{24,32},{32,40},{40,48},{48,56},{56,64},{64,7... | collective-permute-start | bytes 55304 | tf_op jit(solution)/shard_map/ppermute | solution.py:17
  23.3 30.5 %all-to-all-start = ((bf16[128,4,128]{2,1,0:T(4,128)(2,1)}), bf16[128,4,128]{2,1,0:T(4,128)(2,1)S(1)}, u32[]{:S(2)}, u32[]{:S(2)}) async-start(bf16[128,4,128]{2,1,0:T(4,128)(2,1)} %bitcast.2), calls=%async_computation | async-start | bytes 262144 | tf_op jit(solution)/shard_map/all_to_all | solution.py:73
  42.5 105.5 %reduce-scatter.2.cloned.1.call-start = ((), (), s32[]{:S(2)}) async-start(), calls=%async_computation.3 | async-start | bytes 1179648 | tf_op jit(solution)/shard_map/reduce_scatter | solution.py:98
  65.3 104.0 %copy-start.1 = (f32[512]{0:T(512)S(1)}, f32[512]{0:T(512)}, u32[]{:S(2)}) copy-start(f32[512]{0:T(512)} %param.11) | copy-start | bytes 6148
Sparse Core Ops, SparseCore 0:
  86.5 61.3 reduce-scatter.1

commit v2 on v1

--- a/solution.py
+++ b/solution.py
@@ -6,8 +6,9 @@
 from jax.sharding import Mesh, PartitionSpec as P
 
 epsilon = 1e-06
-REDUCE_MODE = "flat"
-TP_AXES = "tp"
+SCATTER_MODE = "a2a_zh"
+TOTAL_MODE = "gather"
+TP_AXES = ("zh", "co")
 highest = lax.Precision.HIGHEST
 
 
@@ -60,6 +61,73 @@
     return signal / length_total
 
 
+def swapped(block, axis, distance):
+    count = lax.axis_size(axis)
+    route = [(i, (i + distance) % count) for i in range(count)]
+    return lax.ppermute(block, axis, route)
+
+
+def ring_scatter(partial_value, group_ch):
+    tok_count = partial_value.shape[0]
+    zh_count = lax.axis_size("zh")
+    zh_index = lax.axis_index("zh")
+    co_index = lax.axis_index("co")
+    blocks = partial_value.reshape(tok_count, zh_count, 2, group_ch)
+    mine = lax.dynamic_index_in_dim(blocks, co_index, 2, keepdims=False)
+    other = lax.dynamic_index_in_dim(blocks, 1 - co_index, 2, keepdims=False)
+    acc = mine + swapped(other.astype(jnp.bfloat16), "co", 1).astype(jnp.float32)
+    if SCATTER_MODE == "a2a_tp":
+        order = blocks.transpose(1, 2, 0, 3).astype(jnp.bfloat16)
+        got = lax.all_to_all(order.reshape(zh_count * 2, tok_count, group_ch), TP_AXES, 0, 0, tiled=True)
+        return jnp.sum(got.astype(jnp.float32), axis=0)
+    if SCATTER_MODE == "a2a_zh":
+        order = acc.transpose(1, 0, 2).astype(jnp.bfloat16)
+        got = lax.all_to_all(order, "zh", 0, 0, tiled=True)
+        return mine_total(got, acc, zh_index)
+    if SCATTER_MODE == "direct":
+        total = lax.dynamic_index_in_dim(acc, zh_index, 1, keepdims=False)
+        for distance in range(1, zh_count):
+            chunk = lax.dynamic_index_in_dim(acc, (zh_index + distance) % zh_count, 1, keepdims=False)
+            total = total + swapped(chunk.astype(jnp.bfloat16), "zh", distance).astype(jnp.float32)
+        return total
+    half = group_ch // 2
+    ahead = acc[:, :, :half]
+    behind = acc[:, :, half:]
+    send_a = lax.dynamic_index_in_dim(ahead, (zh_index - 1) % zh_count, 1, keepdims=False)
+    send_b = lax.dynamic_index_in_dim(behind, (zh_index + 1) % zh_count, 1, keepdims=False)
+    for step in range(zh_count - 1):
+        got_a = swapped(send_a.astype(jnp.bfloat16), "zh", 1).astype(jnp.float32)
+        got_b = swapped(send_b.astype(jnp.bfloat16), "zh", zh_count - 1).astype(jnp.float32)
+        send_a = got_a + lax.dynamic_index_in_dim(ahead, (zh_index - step - 2) % zh_count, 1, keepdims=False)
+        send_b = got_b + lax.dynamic_index_in_dim(behind, (zh_index + step + 2) % zh_count, 1, keepdims=False)
+    return jnp.concatenate([send_a, send_b], axis=1)
+
+
+def mine_total(got, acc, zh_index):
+    own = lax.dynamic_index_in_dim(acc, zh_index, 1, keepdims=False)
+    count = got.shape[0]
+    total = own
+    for source in range(count):
+        keep = jnp.where(source == zh_index, 0.0, 1.0).astype(jnp.float32)
+        total = total + keep * got[source].astype(jnp.float32)
+    return total
+
+
+def row_total(values):
+    if TOTAL_MODE == "psum":
+        return lax.psum(values, TP_AXES)
+    if TOTAL_MODE == "gather":
+        return jnp.sum(lax.all_gather(values, TP_AXES, axis=0, tiled=False), axis=0)
+    total = values + swapped(values, "co", 1)
+    zh_count = lax.axis_size("zh")
+    step = 1
+    while step < zh_count:
+        route = [(i, i ^ step) for i in range(zh_count)]
+        total = total + lax.ppermute(total, "zh", route)
+        step *= 2
+    return total
+
+
 def body(projected, short_taps, long_filter, out_weight, residual, norm_gain):
     tap_count = short_taps.shape[1]
     tok_rows = projected.shape[2]
@@ -94,21 +162,11 @@
     )
     tok_count, col_count = partial_value.shape
     group_ch = out_weight.shape[0]
-    if REDUCE_MODE == "flat":
-        own_part = lax.psum_scatter(
-            partial_value.astype(jnp.bfloat16), TP_AXES, scatter_dimension=1, tiled=True
-        )
-    else:
-        zh_count = lax.axis_size("zh")
-        co_count = lax.axis_size("co")
-        blocks = partial_value.astype(jnp.bfloat16).reshape(tok_count, zh_count, co_count, group_ch)
-        blocks = blocks.transpose(0, 2, 1, 3).reshape(tok_count, col_count)
-        half_part = lax.psum_scatter(blocks, "co", scatter_dimension=1, tiled=True)
-        own_part = lax.psum_scatter(half_part, "zh", scatter_dimension=1, tiled=True)
+    own_part = ring_scatter(partial_value, group_ch)
     start_col = lax.axis_index(TP_AXES) * group_ch
     own_res = lax.dynamic_slice_in_dim(residual, start_col, group_ch, 1)
     own_rows = own_res.astype(jnp.float32) + own_part.astype(jnp.float32)
-    square_sum = lax.psum(jnp.sum(own_rows * own_rows, axis=1), TP_AXES)
+    square_sum = row_total(jnp.sum(own_rows * own_rows, axis=1))
     inverse_rms = lax.rsqrt(square_sum / col_count + epsilon)
     residual_out = own_rows.astype(jnp.bfloat16)
     normed_out = (own_rows * inverse_rms[:, None] * norm_gain[None, :]).astype(jnp.bfloat16)

time: 178 us -> 154 us (0.87)
  starting transfers between devices: 23.3 us -> 51.2 us
  waiting for transfers between devices: 71 us -> 44.8 us
  blocking collectives: 37.2 us -> 16.2 us
  between operations: 14.3 us -> 0.91 us
  local copies, waits for them, and re-layouts: 1.41 us -> 8.62 us
    reduce_scatter x1 -> x0, waiting for transfers between devices: 61.6 us -> none  [body(): lax.psum_scatter(partial_value.astype(jnp.bfloat16), TP_AXES, scatter_dim...]
    all_to_all x0 -> x2, waiting for transfers between devices: none -> 33.6 us  [the longest x1 28.7 us: ring_scatter(): got = lax.all_to_all(order, 'zh', 0, 0, tiled=True)]
    all_to_all x0 -> x2, starting transfers between devices: none -> 21.9 us  [the longest x1 15.7 us: ring_scatter(): got = lax.all_to_all(order, 'zh', 0, 0, tiled=True)]
    psum x1 -> x0, blocking collectives: 20.2 us -> none  [body(): square_sum = lax.psum(jnp.sum(own_rows * own_rows, axis=1), TP_AXES)]
    all_to_all x1 -> x0, blocking collectives: 17 us -> none  [body(): lax.all_to_all(conv, 'ctx', split_axis=1, concat_axis=0, tiled=True)]
    all_gather x0 -> x1, blocking collectives: none -> 16.2 us  [row_total(): return jnp.sum(lax.all_gather(values, TP_AXES, axis=0, tiled=False), axis=0)]
    dot_general x0 -> x1, local copies, waits for them, and re-layouts: none -> 6.49 us  [body(): lax.dot_general(gated, out_weight, (((0,), (0,)), ((), ())), preferred_el...]
    ppermute x0 -> x1, starting transfers between devices: none -> 5.99 us  [swapped(): return lax.ppermute(block, axis, route)]
  transfers between devices with their start and end apart: 3 -> 5, of which waited for: 2 -> 4; matrix products, arithmetic and copies ran while one was open for 5% -> 10% of each run, Pallas kernels for 0% -> 0%
where the time goes in v2:
time: 154 us; the launch traced here: 153 us
  starting transfers between devices  51.2 us (33%)
  waiting for transfers between devices  44.8 us (29%)
  matrix products  22.5 us (15%)
  blocking collectives  16.2 us (11%)
  other arithmetic  9.11 us (6%)
  local copies, waits for them, and re-layouts  8.62 us (6%)
    all_to_all x1, waiting for transfers between devices, ring_scatter(): got = lax.all_to_all(order, 'zh', 0, 0, tiled=True)  28.7 us
    all_to_all x1, starting transfers between devices, body(): lax.all_to_all(product, 'ctx', split_axis=0, concat_axis=1, tiled=True)  19.3 us
    dot_general x18, matrix products, contract(): return jnp.einsum(form, first_arg, second_arg, precision=highest)  18.8 us
    all_gather x1, blocking collectives, row_total(): return jnp.sum(lax.all_gather(values, TP_AXES, axis=0, tiled=False), axis=0)  16.2 us
    all_to_all x1, starting transfers between devices, ring_scatter(): got = lax.all_to_all(order, 'zh', 0, 0, tiled=True)  15.7 us
    all_to_all x1, waiting for transfers between devices, body(): lax.all_to_all(product, 'ctx', split_axis=0, concat_axis=1, tiled=True)  9.52 us
    dot_general x1, local copies, waits for them, and re-layouts, body(): lax.dot_general(gated, out_weight, (((0,), (0,)), ((), ())), preferred_el...  6.49 us
    all_to_all x1, starting transfers between devices, body(): lax.all_to_all(conv, 'ctx', split_axis=1, concat_axis=0, tiled=True)  6.17 us
  transfers between devices with their start and end apart: 5, of which 4 were waited for; matrix products, arithmetic and copies ran while one was open for 10% of the time, Pallas kernels for 0%

profile of v2, /device:TPU:1, one launch (start us, length us, event | category | flops | bytes accessed | tf_op | source)
XLA Modules:
  0.0 153.2 jit_solution(17227173175740611402)
XLA Ops:
  0.6 1.2 slice.64
  1.9 4.0 %collective-permute-start = (bf16[3,512,6]{2,1,0:T(8,128)(2,1)S(1)}, bf16[3,512,6]{2,1,0:T(8,128)(2,1)S(1)}, u32[]{:S(2)}, u32[]{:S(2)}) collective-permute-start(bf16[3,512,6]{2,1,0:T(8,128)(2,1)S(1)} %slice.64), channel_id=1, source_target_pairs={{0,8},{8,16},{16,24},{24,32},{32,40},{40,48},{48,56},{56,64},{64,7... | collective-permute-start | bytes 55304 | tf_op jit(solution)/shard_map/ppermute | solution.py:18
  6.4 2.0 %convolution_negate_fusion = f32[256,4,128]{2,0,1:T(8,128)S(1)} fusion(f32[1,4,128,128]{3,1,2,0:T(4,128)} %bitcast.145), kind=kOutput, calls=%fused_computation | convolution fusion | flops 201916416 | bytes 786432 | tf_op jit(solution)/shard_map/cma,mk->cka/dot_general | solution.py:30
  8.4 2.0 %fusion.29 = f32[256,4,128]{2,0,1:T(8,128)S(1)} fusion(f32[1,4,128,128]{3,1,2,0:T(4,128)} %bitcast.146), kind=kOutput, calls=%fused_computation.59 | convolution fusion | flops 201785344 | bytes 786432 | tf_op jit(solution)/shard_map/cma,mk->cka/dot_general | solution.py:30
  10.5 1.0 slice_convert_fusion.6
  11.5 0.8 fusion.8
  12.3 0.8 convolution_add_fusion.1
  13.2 2.9 %multiply_add_fusion = f32[3,512,128]{2,1,0:T(8,128)S(1)} fusion(bf16[3,512,128]{2,1,0:T(8,128)(2,1)S(1)} %copy-done, bf16[3,512,6]{2,1,0:T(8,128)(2,1)S(1)} %collective-permute-done, f32[3,512]{1,0:T(4,128)S(1)} %get-tuple-element.19, f32[3,512]{1,0:T(4,128)S(1)} %get-tuple-element.20, f32[3,512]{1,0:T(4,128)S(1)} %get-tuple-element.21, ...), kind=kLoop, calls=%fused_computation.24 | loop fusion | flops 7471104 | bytes 1241088 | tf_op jit(solution)/shard_map/add | solution.py:139
  16.8 19.3 %all-to-all-start = ((bf16[128,4,128]{2,1,0:T(4,128)(2,1)}), bf16[128,4,128]{2,1,0:T(4,128)(2,1)S(1)}, u32[]{:S(2)}, u32[]{:S(2)}) async-start(bf16[128,4,128]{2,1,0:T(4,128)(2,1)} %bitcast.1), calls=%async_computation | async-start | bytes 262144 | tf_op jit(solution)/shard_map/all_to_all | solution.py:141
  36.1 0.8 fusion.4
  36.9 0.8 convolution_subtract_fusion.1
  37.8 9.5 %all-to-all-done = bf16[128,4,128]{2,1,0:T(4,128)(2,1)S(1)} async-done(((bf16[128,4,128]{2,1,0:T(4,128)(2,1)}), bf16[128,4,128]{2,1,0:T(4,128)(2,1)S(1)}, u32[]{:S(2)}, u32[]{:S(2)}) %all-to-all-start) | async-done | bytes 131104 | tf_op jit(solution)/shard_map/all_to_all | solution.py:141
  47.3 0.9 convolution_negate_fusion.1
  48.2 0.9 fusion.53
  49.1 0.8 fusion.14
  49.9 0.8 fusion.10
  50.7 0.8 convolution_add_fusion.2
  51.6 0.9 multiply_subtract_fusion
  54.1 0.8 convolution_subtract_fusion
  55.7 1.4 fusion.19
  57.1 1.6 %fusion.2 = bf16[4,128,128]{1,2,0:T(8,128)(2,1)S(1)} fusion(f32[4,128,128]{2,1,0:T(8,128)S(1)} %fusion.19, f32[4,256,128]{2,1,0:T(8,128)S(1)} %convolution_subtract_fusion, f32[4,256,128]{2,1,0:T(8,128)S(1)} %convolution_add_fusion, f32[256,128]{1,0:T(8,128)S(1)} %get-tuple-element.17, f32[256,128]{1,0:T(8,128)S(1)} %get-tuple-element.18), kind=kOutput, calls=%fused_computation.21 | convolution fusion | flops 202375168 | bytes 1703936 | tf_op jit(solution)/shard_map/mk,cka->cma/dot_general | solution.py:30
  59.6 6.2 %all-to-all-start.1 = ((bf16[4,128,128]{2,0,1:T(4,128)(2,1)}), bf16[4,128,128]{2,0,1:T(4,128)(2,1)S(1)}, u32[]{:S(2)}, u32[]{:S(2)}) async-start(bf16[4,128,128]{2,0,1:T(4,128)(2,1)} %copy.33), calls=%async_computation.1 | async-start | bytes 262144 | tf_op jit(solution)/shard_map/all_to_all | solution.py:158
  65.7 6.5 %copy.48 = bf16[4096,512]{1,0:T(8,128)(2,1)} copy(bf16[4096,512]{0,1:T(8,128)(2,1)} %bitcast.144) | data formatting | bytes 8388608 | tf_op jit(solution)/shard_map/dot_general | solution.py:160
  72.2 4.9 %all-to-all-done.1 = bf16[4,128,128]{2,0,1:T(4,128)(2,1)S(1)} async-done(((bf16[4,128,128]{2,0,1:T(4,128)(2,1)}), bf16[4,128,128]{2,0,1:T(4,128)(2,1)S(1)}, u32[]{:S(2)}, u32[]{:S(2)}) %all-to-all-start.1) | async-done | bytes 131104 | tf_op jit(solution)/shard_map/all_to_all | solution.py:158
  77.1 3.7 %fusion.47 = f32[128,4,2,512]{3,0,2,1:T(8,128)S(1)} fusion(bf16[4,2,512,512]{3,2,1,0:T(8,128)(2,1)} %bitcast.143, f32[1,512,128]{2,1,0:T(8,128)S(1)} %bitcast.147, f32[3,512,128]{2,1,0:T(8,128)S(1)} %multiply_add_fusion), kind=kOutput, calls=%fused_computation.91 | convolution fusion | flops 537001984 | bytes 6815744 | tf_op jit(solution)/shard_map/dot_general | solution.py:160
  80.9 6.0 %collective-permute-start.1 = (bf16[128,4,512]{2,0,1:T(8,128)(2,1)S(1)}, bf16[128,4,512]{2,0,1:T(8,128)(2,1)}, u32[]{:S(2)}, u32[]{:S(2)}) collective-permute-start(bf16[128,4,512]{2,0,1:T(8,128)(2,1)S(1)} %fusion.3), channel_id=1, source_target_pairs={{0,1},{1,0},{2,3},{3,2},{4,5},{5,4},{6,7},{7,6},{8,9},{9,8},{10,11... | collective-permute-start | bytes 1572872 | tf_op jit(solution)/shard_map/ppermute | solution.py:67
  86.9 1.6 %collective-permute-done.1 = bf16[128,4,512]{2,0,1:T(8,128)(2,1)} collective-permute-done((bf16[128,4,512]{2,0,1:T(8,128)(2,1)S(1)}, bf16[128,4,512]{2,0,1:T(8,128)(2,1)}, u32[]{:S(2)}, u32[]{:S(2)}) %collective-permute-start.1) | collective-permute-done | bytes 524320 | tf_op jit(solution)/shard_map/ppermute | solution.py:67
  88.6 2.1 %convert_bitcast_fusion = (bf16[4,128,512]{2,1,0:T(8,128)(2,1)}, f32[128,4,512]{2,0,1:T(8,128)S(1)}) fusion(bf16[128,4,512]{2,0,1:T(8,128)(2,1)} %collective-permute-done.1, f32[128,4,2,512]{3,0,2,1:T(8,128)S(1)} %fusion.47, s32[]{:T(128)S(6)} %select_n.111), kind=kLoop, calls=%fused_computation.38 | loop fusion | flops 786432 | bytes 3145732 | tf_op jit(solution)/shard_map/convert_element_type | solution.py:84
  90.7 15.7 %all-to-all-start.2 = ((bf16[4,128,512]{2,1,0:T(8,128)(2,1)}), bf16[4,128,512]{2,1,0:T(8,128)(2,1)S(1)}, u32[]{:S(2)}, u32[]{:S(2)}) async-start(bf16[4,128,512]{2,1,0:T(8,128)(2,1)} %get-tuple-element.4), calls=%async_computation.2 | async-start | bytes 1048576 | tf_op jit(solution)/shard_map/all_to_all | solution.py:85
  106.4 28.7 %all-to-all-done.2 = bf16[4,128,512]{2,1,0:T(8,128)(2,1)S(1)} async-done(((bf16[4,128,512]{2,1,0:T(8,128)(2,1)}), bf16[4,128,512]{2,1,0:T(8,128)(2,1)S(1)}, u32[]{:S(2)}, u32[]{:S(2)}) %all-to-all-start.2) | async-done | bytes 524320 | tf_op jit(solution)/shard_map/all_to_all | solution.py:85
  135.1 1.1 multiply_reduce_fusion
  136.2 16.2 %all-gather.1 = f32[8,1,128]{2,1,0:T(1,128)S(1)} all-gather(f32[1,1,128]{2,1,0:T(1,128)S(1)} %bitcast.149), channel_id=2, replica_groups=mesh['ctx'=128,'zh'=4,'co'=2] {'zh','co'}, dimensions={0}, use_global_device_ids=true | all-gather | bytes 4608 | tf_op jit(solution)/shard_map/all_gather | solution.py:120
  (20 shorter events, 5.4 us)
Async XLA Ops:
  0.6 12.6 %copy-start = (bf16[3,512,128]{2,1,0:T(8,128)(2,1)S(1)}, bf16[3,512,128]{2,1,0:T(8,128)(2,1)}, u32[]{:S(2)}) copy-start(bf16[3,512,128]{2,1,0:T(8,128)(2,1)} %param.6) | copy-start | bytes 1179652
  1.9 11.4 %collective-permute-start = (bf16[3,512,6]{2,1,0:T(8,128)(2,1)S(1)}, bf16[3,512,6]{2,1,0:T(8,128)(2,1)S(1)}, u32[]{:S(2)}, u32[]{:S(2)}) collective-permute-start(bf16[3,512,6]{2,1,0:T(8,128)(2,1)S(1)} %slice.64), channel_id=1, source_target_pairs={{0,8},{8,16},{16,24},{24,32},{32,40},{40,48},{48,56},{56,64},{64,7... | collective-permute-start | bytes 55304 | tf_op jit(solution)/shard_map/ppermute | solution.py:18
  16.8 30.5 %all-to-all-start = ((bf16[128,4,128]{2,1,0:T(4,128)(2,1)}), bf16[128,4,128]{2,1,0:T(4,128)(2,1)S(1)}, u32[]{:S(2)}, u32[]{:S(2)}) async-start(bf16[128,4,128]{2,1,0:T(4,128)(2,1)} %bitcast.1), calls=%async_computation | async-start | bytes 262144 | tf_op jit(solution)/shard_map/all_to_all | solution.py:141
  59.6 17.5 %all-to-all-start.1 = ((bf16[4,128,128]{2,0,1:T(4,128)(2,1)}), bf16[4,128,128]{2,0,1:T(4,128)(2,1)S(1)}, u32[]{:S(2)}, u32[]{:S(2)}) async-start(bf16[4,128,128]{2,0,1:T(4,128)(2,1)} %copy.33), calls=%async_computation.1 | async-start | bytes 262144 | tf_op jit(solution)/shard_map/all_to_all | solution.py:158
  80.8 71.6 %copy-start.1 = (f32[512]{0:T(512)S(1)}, f32[512]{0:T(512)}, u32[]{:S(2)}) copy-start(f32[512]{0:T(512)} %param.11) | copy-start | bytes 6148
  80.9 7.6 %collective-permute-start.1 = (bf16[128,4,512]{2,0,1:T(8,128)(2,1)S(1)}, bf16[128,4,512]{2,0,1:T(8,128)(2,1)}, u32[]{:S(2)}, u32[]{:S(2)}) collective-permute-start(bf16[128,4,512]{2,0,1:T(8,128)(2,1)S(1)} %fusion.3), channel_id=1, source_target_pairs={{0,1},{1,0},{2,3},{3,2},{4,5},{5,4},{6,7},{7,6},{8,9},{9,8},{10,11... | collective-permute-start | bytes 1572872 | tf_op jit(solution)/shard_map/ppermute | solution.py:67
  90.7 44.5 %all-to-all-start.2 = ((bf16[4,128,512]{2,1,0:T(8,128)(2,1)}), bf16[4,128,512]{2,1,0:T(8,128)(2,1)S(1)}, u32[]{:S(2)}, u32[]{:S(2)}) async-start(bf16[4,128,512]{2,1,0:T(8,128)(2,1)} %get-tuple-element.4), calls=%async_computation.2 | async-start | bytes 1048576 | tf_op jit(solution)/shard_map/all_to_all | solution.py:85

commit v3 on v2

--- a/solution.py
+++ b/solution.py
@@ -162,7 +162,17 @@
     )
     tok_count, col_count = partial_value.shape
     group_ch = out_weight.shape[0]
-    own_part = ring_scatter(partial_value, group_ch)
+    half_cols = group_ch // 2
+    weight_blocks = out_weight.reshape(group_ch, col_count // group_ch, group_ch)
+    pieces = []
+    for piece in range(2):
+        weight_piece = weight_blocks[:, :, piece * half_cols : (piece + 1) * half_cols]
+        piece_value = lax.dot_general(
+            gated, weight_piece.reshape(group_ch, -1), (((0,), (0,)), ((), ())),
+            preferred_element_type=jnp.float32,
+        )
+        pieces.append(ring_scatter(piece_value, half_cols))
+    own_part = jnp.concatenate(pieces, axis=1)
     start_col = lax.axis_index(TP_AXES) * group_ch
     own_res = lax.dynamic_slice_in_dim(residual, start_col, group_ch, 1)
     own_rows = own_res.astype(jnp.float32) + own_part.astype(jnp.float32)

time: 154 us -> 163 us (1.058)
  starting transfers between devices: 51.2 us -> 60.9 us
  waiting for transfers between devices: 44.8 us -> 36.7 us
  local copies, waits for them, and re-layouts: 8.62 us -> 14.7 us
  matrix products: 22.5 us -> 20.4 us
    slice x0 -> x3, local copies, waits for them, and re-layouts: none -> 8.23 us  [body(): weight_blocks[:, :, piece * half_cols:(piece + 1) * half_cols]]
    all_to_all x1 -> x2, starting transfers between devices: 15.7 us -> 22.3 us  [ring_scatter(): got = lax.all_to_all(order, 'zh', 0, 0, tiled=True)]
    dot_general x1 -> x0, local copies, waits for them, and re-layouts: 6.49 us -> none  [body(): lax.dot_general(gated, out_weight, (((0,), (0,)), ((), ())), preferred_el...]
    all_to_all x1 -> x2, waiting for transfers between devices: 28.7 us -> 24.2 us  [ring_scatter(): got = lax.all_to_all(order, 'zh', 0, 0, tiled=True)]
    unnamed x8 -> x11, local copies, waits for them, and re-layouts: 0.03 us -> 4.46 us
    all_to_all x1, waiting for transfers between devices: 4.87 us -> 1.69 us  [body(): lax.all_to_all(conv, 'ctx', split_axis=1, concat_axis=0, tiled=True)]
    ppermute x1 -> x2, starting transfers between devices: 5.99 us -> 8.21 us  [swapped(): return lax.ppermute(block, axis, route)]
    dot_general x1 -> x2, matrix products: 3.7 us -> 1.62 us  [body(): lax.dot_general(gated, weight_piece.reshape(group_ch, -1), (((0,), (0,)),...]
  transfers between devices with their start and end apart: 5 -> 7, of which waited for: 4 -> 5; matrix products, arithmetic and copies ran while one was open for 10% -> 14% of each run, Pallas kernels for 0% -> 0%
where the time goes in v3:
time: 163 us; the launch traced here: 161 us
  starting transfers between devices  60.9 us (37%)
  waiting for transfers between devices  36.7 us (23%)
  matrix products  20.4 us (13%)
  blocking collectives  16.7 us (10%)
  local copies, waits for them, and re-layouts  14.7 us (9%)
  other arithmetic  10.6 us (7%)
    all_to_all x2, waiting for transfers between devices, ring_scatter(): got = lax.all_to_all(order, 'zh', 0, 0, tiled=True)  24.2 us
    all_to_all x2, starting transfers between devices, ring_scatter(): got = lax.all_to_all(order, 'zh', 0, 0, tiled=True)  22.3 us
    all_to_all x1, starting transfers between devices, body(): lax.all_to_all(product, 'ctx', split_axis=0, concat_axis=1, tiled=True)  20.3 us
    dot_general x18, matrix products, contract(): return jnp.einsum(form, first_arg, second_arg, precision=highest)  18.8 us
    all_gather x1, blocking collectives, row_total(): return jnp.sum(lax.all_gather(values, TP_AXES, axis=0, tiled=False), axis=0)  16.7 us
    all_to_all x1, waiting for transfers between devices, body(): lax.all_to_all(product, 'ctx', split_axis=0, concat_axis=1, tiled=True)  9.51 us
    slice x3, local copies, waits for them, and re-layouts, body(): weight_blocks[:, :, piece * half_cols:(piece + 1) * half_cols]  8.23 us
    ppermute x2, starting transfers between devices, swapped(): return lax.ppermute(block, axis, route)  8.21 us
  transfers between devices with their start and end apart: 7, of which 5 were waited for; matrix products, arithmetic and copies ran while one was open for 14% of the time, Pallas kernels for 0%

profile of v3, /device:TPU:1, one launch (start us, length us, event | category | flops | bytes accessed | tf_op | source)
XLA Modules:
  0.0 161.0 jit_solution(9685686452427905137)
XLA Ops:
  0.6 1.2 slice.82
  1.8 4.0 %collective-permute-start = (bf16[3,512,6]{2,1,0:T(8,128)(2,1)S(1)}, bf16[3,512,6]{2,1,0:T(8,128)(2,1)S(1)}, u32[]{:S(2)}, u32[]{:S(2)}) collective-permute-start(bf16[3,512,6]{2,1,0:T(8,128)(2,1)S(1)} %slice.82), channel_id=1, source_target_pairs={{0,8},{8,16},{16,24},{24,32},{32,40},{40,48},{48,56},{56,64},{64,7... | collective-permute-start | bytes 55304 | tf_op jit(solution)/shard_map/ppermute | solution.py:18
  6.3 2.0 %convolution_negate_fusion = f32[256,4,128]{2,0,1:T(8,128)S(1)} fusion(f32[1,4,128,128]{3,1,2,0:T(4,128)} %bitcast.180), kind=kOutput, calls=%fused_computation | convolution fusion | flops 201916416 | bytes 786432 | tf_op jit(solution)/shard_map/cma,mk->cka/dot_general | solution.py:30
  8.4 2.0 %fusion.30 = f32[256,4,128]{2,0,1:T(8,128)S(1)} fusion(f32[1,4,128,128]{3,1,2,0:T(4,128)} %bitcast.181), kind=kOutput, calls=%fused_computation.61 | convolution fusion | flops 201785344 | bytes 786432 | tf_op jit(solution)/shard_map/cma,mk->cka/dot_general | solution.py:30
  12.2 2.9 %multiply_add_fusion = f32[3,512,128]{2,1,0:T(8,128)S(1)} fusion(bf16[3,512,128]{2,1,0:T(8,128)(2,1)S(1)} %copy-done, bf16[3,512,6]{2,1,0:T(8,128)(2,1)S(1)} %collective-permute-done, f32[3,512]{1,0:T(4,128)S(1)} %get-tuple-element.21, f32[3,512]{1,0:T(4,128)S(1)} %get-tuple-element.22, f32[3,512]{1,0:T(4,128)S(1)} %get-tuple-element.23, ...), kind=kLoop, calls=%fused_computation.22 | loop fusion | flops 7471104 | bytes 1241088 | tf_op jit(solution)/shard_map/add | solution.py:139
  15.8 20.3 %all-to-all-start = ((bf16[128,4,128]{2,1,0:T(4,128)(2,1)}), bf16[128,4,128]{2,1,0:T(4,128)(2,1)S(1)}, u32[]{:S(2)}, u32[]{:S(2)}) async-start(bf16[128,4,128]{2,1,0:T(4,128)(2,1)} %bitcast.1), calls=%async_computation | async-start | bytes 262144 | tf_op jit(solution)/shard_map/all_to_all | solution.py:141
  36.9 0.8 convolution_subtract_fusion.1
  37.7 9.5 %all-to-all-done = bf16[128,4,128]{2,1,0:T(4,128)(2,1)S(1)} async-done(((bf16[128,4,128]{2,1,0:T(4,128)(2,1)}), bf16[128,4,128]{2,1,0:T(4,128)(2,1)S(1)}, u32[]{:S(2)}, u32[]{:S(2)}) %all-to-all-start) | async-done | bytes 131104 | tf_op jit(solution)/shard_map/all_to_all | solution.py:141
  47.2 0.9 convolution_negate_fusion.1
  48.1 0.9 fusion.51
  50.7 0.8 convolution_add_fusion.2
  51.5 0.9 multiply_subtract_fusion
  55.7 1.4 fusion.18
  57.1 1.6 %fusion.2 = bf16[4,128,128]{1,2,0:T(8,128)(2,1)S(1)} fusion(f32[4,128,128]{2,1,0:T(8,128)S(1)} %fusion.18, f32[4,256,128]{2,1,0:T(8,128)S(1)} %convolution_subtract_fusion, f32[4,256,128]{2,1,0:T(8,128)S(1)} %convolution_add_fusion, f32[256,128]{1,0:T(8,128)S(1)} %get-tuple-element.19, f32[256,128]{1,0:T(8,128)S(1)} %get-tuple-element.20), kind=kOutput, calls=%fused_computation.21 | convolution fusion | flops 202375168 | bytes 1703936 | tf_op jit(solution)/shard_map/mk,cka->cma/dot_general | solution.py:30
  59.5 6.2 %all-to-all-start.1 = ((bf16[4,128,128]{2,0,1:T(4,128)(2,1)}), bf16[4,128,128]{2,0,1:T(4,128)(2,1)S(1)}, u32[]{:S(2)}, u32[]{:S(2)}) async-start(bf16[4,128,128]{2,0,1:T(4,128)(2,1)} %copy.39), calls=%async_computation.1 | async-start | bytes 262144 | tf_op jit(solution)/shard_map/all_to_all | solution.py:158
  65.7 4.4 %copy.68 = bf16[64,8,8,512]{3,2,1,0:T(8,128)(2,1)S(1)} copy(bf16[64,8,8,512]{3,1,2,0:T(8,128)(2,1)} %bitcast.179) | data formatting | bytes 8388608
  70.1 2.2 %fusion.181 = (bf16[512,8,256]{2,1,0:T(8,128)(2,1)}, bf16[512,8,256]{2,1,0:T(8,128)(2,1)}) fusion(bf16[512,8,512]{2,1,0:T(8,128)(2,1)S(1)} %bitcast.176), kind=kLoop, calls=%fused_computation.233 | loop fusion | bytes 8388608 | tf_op jit(solution)/shard_map/slice | solution.py:169
  72.3 3.0 %copy.40 = bf16[512,8,256]{0,2,1:T(8,128)(2,1)S(1)} copy(bf16[512,8,256]{2,1,0:T(8,128)(2,1)} %get-tuple-element.6) | data formatting | bytes 4194304 | tf_op jit(solution)/shard_map/slice | solution.py:169
  75.3 1.7 %all-to-all-done.1 = bf16[4,128,128]{2,0,1:T(4,128)(2,1)S(1)} async-done(((bf16[4,128,128]{2,0,1:T(4,128)(2,1)}), bf16[4,128,128]{2,0,1:T(4,128)(2,1)S(1)}, u32[]{:S(2)}, u32[]{:S(2)}) %all-to-all-start.1) | async-done | bytes 131104 | tf_op jit(solution)/shard_map/all_to_all | solution.py:158
  78.0 6.0 %collective-permute-start.1 = (bf16[128,4,256]{2,0,1:T(8,128)(2,1)S(1)}, bf16[128,4,256]{2,0,1:T(8,128)(2,1)}, u32[]{:S(2)}, u32[]{:S(2)}) collective-permute-start(bf16[128,4,256]{2,0,1:T(8,128)(2,1)S(1)} %fusion.27), channel_id=1, source_target_pairs={{0,1},{1,0},{2,3},{3,2},{4,5},{5,4},{6,7},{7,6},{8,9},{9,8},{10,11... | collective-permute-start | bytes 786440 | tf_op jit(solution)/shard_map/ppermute | solution.py:67
  84.0 3.0 %copy.42 = bf16[512,8,256]{0,2,1:T(8,128)(2,1)S(1)} copy(bf16[512,8,256]{2,1,0:T(8,128)(2,1)} %get-tuple-element.7) | data formatting | bytes 4194304 | tf_op jit(solution)/shard_map/slice | solution.py:169
  87.0 1.9 %convert_bitcast_fusion.1 = (bf16[4,128,256]{2,1,0:T(8,128)(2,1)}, f32[128,4,256]{2,0,1:T(8,128)}) fusion(bf16[128,4,256]{2,0,1:T(8,128)(2,1)} %collective-permute-done.1, f32[128,4,2,256]{3,0,2,1:T(8,128)S(1)} %fusion.182, s32[]{:T(128)S(6)} %select_n.118), kind=kLoop, calls=%fused_computation.71 | loop fusion | flops 393216 | bytes 1572868 | tf_op jit(solution)/shard_map/convert_element_type | solution.py:84
  88.9 15.7 %all-to-all-start.2 = ((bf16[4,128,256]{2,1,0:T(8,128)(2,1)}), bf16[4,128,256]{2,1,0:T(8,128)(2,1)S(1)}, u32[]{:S(2)}, u32[]{:S(2)}) async-start(bf16[4,128,256]{2,1,0:T(8,128)(2,1)} %get-tuple-element.2), calls=%async_computation.2 | async-start | bytes 524288 | tf_op jit(solution)/shard_map/all_to_all | solution.py:85
  105.5 2.2 %collective-permute-start.2 = (bf16[128,4,256]{2,0,1:T(8,128)(2,1)S(1)}, bf16[128,4,256]{2,0,1:T(8,128)(2,1)S(1)}, u32[]{:S(2)}, u32[]{:S(2)}) collective-permute-start(bf16[128,4,256]{2,0,1:T(8,128)(2,1)S(1)} %fusion.28), channel_id=1, source_target_pairs={{0,1},{1,0},{2,3},{3,2},{4,5},{5,4},{6,7},{7,6},{8,9},{9,8},{10,11... | collective-permute-start | bytes 786440 | tf_op jit(solution)/shard_map/ppermute | solution.py:67
  107.7 1.2 collective-permute-done.2
  109.8 10.7 %all-to-all-done.2 = bf16[4,128,256]{2,1,0:T(8,128)(2,1)S(1)} async-done(((bf16[4,128,256]{2,1,0:T(8,128)(2,1)}), bf16[4,128,256]{2,1,0:T(8,128)(2,1)S(1)}, u32[]{:S(2)}, u32[]{:S(2)}) %all-to-all-start.2) | async-done | bytes 262176 | tf_op jit(solution)/shard_map/all_to_all | solution.py:85
  120.5 6.6 %all-to-all-start.3 = ((bf16[4,128,256]{2,1,0:T(8,128)(2,1)}), bf16[4,128,256]{2,1,0:T(8,128)(2,1)S(1)}, u32[]{:S(2)}, u32[]{:S(2)}) async-start(bf16[4,128,256]{2,1,0:T(8,128)(2,1)} %get-tuple-element.4), calls=%async_computation.3 | async-start | bytes 524288 | tf_op jit(solution)/shard_map/all_to_all | solution.py:85
  127.0 1.0 bitcast_add_fusion.6
  128.0 13.5 %all-to-all-done.3 = bf16[4,128,256]{2,1,0:T(8,128)(2,1)S(1)} async-done(((bf16[4,128,256]{2,1,0:T(8,128)(2,1)}), bf16[4,128,256]{2,1,0:T(8,128)(2,1)S(1)}, u32[]{:S(2)}, u32[]{:S(2)}) %all-to-all-start.3) | async-done | bytes 262176 | tf_op jit(solution)/shard_map/all_to_all | solution.py:85
  141.6 1.0 multiply_reduce_fusion
  142.6 16.7 %all-gather.1 = f32[8,1,128]{2,1,0:T(1,128)S(1)} all-gather(f32[1,1,128]{2,1,0:T(1,128)S(1)} %bitcast.184), channel_id=2, replica_groups=mesh['ctx'=128,'zh'=4,'co'=2] {'zh','co'}, dimensions={0}, use_global_device_ids=true | all-gather | bytes 4608 | tf_op jit(solution)/shard_map/all_gather | solution.py:120
  159.3 1.7 %multiply_convert_fusion = (bf16[128,512]{1,0:T(8,128)(2,1)}, bf16[128,512]{1,0:T(8,128)(2,1)}) fusion(f32[512]{0:T(512)S(1)} %copy-done.2, f32[128]{0:T(128)S(1)} %add_rsqrt_fusion, f32[128,256]{1,0:T(8,128)S(1)} %bitcast_add_fusion.2, f32[128,256]{1,0:T(8,128)S(1)} %bitcast_add_fusion.6, bf16[128,4096]{1,0:T(8,128)(2,1)} %param.10, s32[]{:T(128)S(6)} %select_n.114), kind=kLoop, calls=%fused_computation.68 | loop fusion | flops 458752 | bytes 657924 | tf_op jit(solution)/shard_map/convert_element_type | solution.py:182
  (35 shorter events, 12.1 us)
Async XLA Ops:
  0.6 9.8 %copy-start.1 = (bf16[3,7,512]{2,1,0:T(8,128)(2,1)S(1)}, bf16[3,7,512]{2,1,0:T(8,128)(2,1)}, u32[]{:S(2)}) copy-start(bf16[3,7,512]{2,1,0:T(8,128)(2,1)} %param.7) | copy-start | bytes 64516
  1.8 10.4 %collective-permute-start = (bf16[3,512,6]{2,1,0:T(8,128)(2,1)S(1)}, bf16[3,512,6]{2,1,0:T(8,128)(2,1)S(1)}, u32[]{:S(2)}, u32[]{:S(2)}) collective-permute-start(bf16[3,512,6]{2,1,0:T(8,128)(2,1)S(1)} %slice.82), channel_id=1, source_target_pairs={{0,8},{8,16},{16,24},{24,32},{32,40},{40,48},{48,56},{56,64},{64,7... | collective-permute-start | bytes 55304 | tf_op jit(solution)/shard_map/ppermute | solution.py:18
  10.5 1.7 %copy-start = (bf16[3,512,128]{2,1,0:T(8,128)(2,1)S(1)}, bf16[3,512,128]{2,1,0:T(8,128)(2,1)}, u32[]{:S(2)}) copy-start(bf16[3,512,128]{2,1,0:T(8,128)(2,1)} %param.6) | copy-start | bytes 1179652
  15.8 31.5 %all-to-all-start = ((bf16[128,4,128]{2,1,0:T(4,128)(2,1)}), bf16[128,4,128]{2,1,0:T(4,128)(2,1)S(1)}, u32[]{:S(2)}, u32[]{:S(2)}) async-start(bf16[128,4,128]{2,1,0:T(4,128)(2,1)} %bitcast.1), calls=%async_computation | async-start | bytes 262144 | tf_op jit(solution)/shard_map/all_to_all | solution.py:141
  59.5 17.5 %all-to-all-start.1 = ((bf16[4,128,128]{2,0,1:T(4,128)(2,1)}), bf16[4,128,128]{2,0,1:T(4,128)(2,1)S(1)}, u32[]{:S(2)}, u32[]{:S(2)}) async-start(bf16[4,128,128]{2,0,1:T(4,128)(2,1)} %copy.39), calls=%async_computation.1 | async-start | bytes 262144 | tf_op jit(solution)/shard_map/all_to_all | solution.py:158
  78.0 9.0 %collective-permute-start.1 = (bf16[128,4,256]{2,0,1:T(8,128)(2,1)S(1)}, bf16[128,4,256]{2,0,1:T(8,128)(2,1)}, u32[]{:S(2)}, u32[]{:S(2)}) collective-permute-start(bf16[128,4,256]{2,0,1:T(8,128)(2,1)S(1)} %fusion.27), channel_id=1, source_target_pairs={{0,1},{1,0},{2,3},{3,2},{4,5},{5,4},{6,7},{7,6},{8,9},{9,8},{10,11... | collective-permute-start | bytes 786440 | tf_op jit(solution)/shard_map/ppermute | solution.py:67
  88.9 31.5 %all-to-all-start.2 = ((bf16[4,128,256]{2,1,0:T(8,128)(2,1)}), bf16[4,128,256]{2,1,0:T(8,128)(2,1)S(1)}, u32[]{:S(2)}, u32[]{:S(2)}) async-start(bf16[4,128,256]{2,1,0:T(8,128)(2,1)} %get-tuple-element.2), calls=%async_computation.2 | async-start | bytes 524288 | tf_op jit(solution)/shard_map/all_to_all | solution.py:85
  105.5 53.8 %copy-start.2 = (f32[512]{0:T(512)S(1)}, f32[512]{0:T(512)}, u32[]{:S(2)}) copy-start(f32[512]{0:T(512)} %param.11) | copy-start | bytes 6148
  105.5 3.4 %collective-permute-start.2 = (bf16[128,4,256]{2,0,1:T(8,128)(2,1)S(1)}, bf16[128,4,256]{2,0,1:T(8,128)(2,1)S(1)}, u32[]{:S(2)}, u32[]{:S(2)}) collective-permute-start(bf16[128,4,256]{2,0,1:T(8,128)(2,1)S(1)} %fusion.28), channel_id=1, source_target_pairs={{0,1},{1,0},{2,3},{3,2},{4,5},{5,4},{6,7},{7,6},{8,9},{9,8},{10,11... | collective-permute-start | bytes 786440 | tf_op jit(solution)/shard_map/ppermute | solution.py:67
  120.5 21.1 %all-to-all-start.3 = ((bf16[4,128,256]{2,1,0:T(8,128)(2,1)}), bf16[4,128,256]{2,1,0:T(8,128)(2,1)S(1)}, u32[]{:S(2)}, u32[]{:S(2)}) async-start(bf16[4,128,256]{2,1,0:T(8,128)(2,1)} %get-tuple-element.4), calls=%async_computation.3 | async-start | bytes 524288 | tf_op jit(solution)/shard_map/all_to_all | solution.py:85
